TPU v7x, 128 devices: a whole 4x4x4 slice. The times are simulated.
128 devices in a mesh: wide: 32 (over x, y, core), rep: 4 (over z).
Axes of the slice: x: 4, y: 4, z: 4, core: 2. Of those that a mesh axis runs over, the one named last changes fastest.
Arguments:
- passages: bfloat16 [131072, 1024], P(('wide', 'rep')), may hold values from -6 to 6
- cluster_ids: int32 [131072], P(('wide', 'rep')), may hold values from 0 to 524287, as said below
- w_first: bfloat16 [1024, 1024], replicated, may hold values from -0.1875 to 0.1875
- w_second: bfloat16 [1024, 256], replicated, may hold values from -0.1875 to 0.1875
- centroids: bfloat16 [524288, 256], P('wide'), may hold values from -6 to 6
Outputs:
- refreshed: bfloat16 [524288, 256], P(('wide', 'rep'))
- residuals: bfloat16 [131072, 256], P(('wide', 'rep'))
Inputs may be any that keep to these rules, and one draw needn't show every extreme that they name: The owner of a passage is cluster_ids // 16384. Among the 1024 rows of one device (aligned blocks), at most 96 have any one owner; in every draw one owner gets exactly 96 rows from every device's block.
All inputs are finite; a program needn't handle non-finite values.
Results may differ from a plain program's by a relative error of at most 0.015.
Values may be sent and summed in bfloat16 or wider, within the bound.
No kernel may reach another device: no remote copies, remote signals or barrier semaphores. Data moves between devices by JAX's collectives and lax.ppermute only.
A program may use at most 128 MiB of HBM per device.

v0:
```python
import jax
import jax.numpy as jnp
from jax import lax
from jax.sharding import PartitionSpec as P


def refresh(current, summed):
    updated = current.astype(jnp.float32) + summed
    return (
        updated * lax.rsqrt(jnp.mean(updated * updated, axis=-1, keepdims=True) + 1e-06)
    ).astype(jnp.bfloat16)


def body(passages, cluster_ids, w_first, w_second, centroids):
    tok_rows = passages.shape[0]
    owners = lax.axis_size("wide")
    cent_rows = centroids.shape[0]
    emb_width = w_second.shape[1]
    capacity = 3 * tok_rows // owners
    hidden = jax.nn.gelu(
        jnp.dot(passages, w_first, preferred_element_type=jnp.float32), approximate=True
    ).astype(jnp.bfloat16)
    projected = jnp.dot(hidden, w_second, preferred_element_type=jnp.float32)
    embedded = (
        projected * lax.rsqrt(jnp.mean(projected * projected, axis=-1, keepdims=True) + 1e-06)
    ).astype(jnp.bfloat16)
    owner_of = cluster_ids // cent_rows
    local_id = cluster_ids - owner_of * cent_rows
    member = (owner_of[:, None] == jnp.arange(owners, dtype=jnp.int32)[None, :]).astype(jnp.int32)
    before = jnp.cumsum(member, axis=0) - member
    slot_of = jnp.sum(before * member, axis=1)
    target = owner_of * capacity + slot_of
    counts = jnp.sum(member, axis=0)
    starts = jnp.cumsum(counts) - counts
    order = jnp.argsort(owner_of, stable=True)
    slot_index = jnp.arange(capacity, dtype=jnp.int32)[None, :]
    valid = (slot_index < counts[:, None]).reshape(owners * capacity)
    position = jnp.minimum(starts[:, None] + slot_index, tok_rows - 1).reshape(owners * capacity)
    source = order[position]
    outgoing = jnp.where(valid[:, None], embedded[source], jnp.zeros((), jnp.bfloat16))
    out_ids = jnp.where(valid, local_id[source], -1)
    incoming, in_ids = (
        lax.all_to_all(outgoing, "wide", split_axis=0, concat_axis=0, tiled=True),
        lax.all_to_all(out_ids, "wide", split_axis=0, concat_axis=0, tiled=True),
    )
    block_rows = min(cent_rows, 2048)
    block_count = cent_rows // block_rows

    def one_block(block_start):
        row_ids = block_start + jnp.arange(block_rows, dtype=jnp.int32)
        selector = (row_ids[:, None] == in_ids[None, :]).astype(jnp.bfloat16)
        return jnp.dot(selector, incoming, preferred_element_type=jnp.float32)

    block_starts = jnp.arange(block_count, dtype=jnp.int32) * block_rows
    partial_value = lax.map(one_block, block_starts).reshape(cent_rows, emb_width)
    safe_ids = jnp.where(in_ids >= 0, in_ids, 0)
    replicas = lax.axis_size("rep")
    share_rows = cent_rows // replicas
    first_row = lax.axis_index("rep") * share_rows
    summed = lax.psum(partial_value.astype(jnp.bfloat16), "rep").astype(jnp.float32)
    fresh_table = refresh(centroids, summed)
    own_rows = lax.dynamic_slice_in_dim(fresh_table, first_row, share_rows, 0)
    picked = fresh_table[safe_ids]
    returned = lax.all_to_all(picked, "wide", split_axis=0, concat_axis=0, tiled=True)
    gathered_rows = returned[target]
    residuals = (embedded.astype(jnp.float32) - gathered_rows.astype(jnp.float32)).astype(
        jnp.bfloat16
    )
    return (own_rows, residuals)


def solution(mesh):
    return jax.shard_map(
        body,
        mesh=mesh,
        in_specs=(P(("wide", "rep"), None), P(("wide", "rep")), P(), P(), P("wide", None)),
        out_specs=(P(("wide", "rep"), None), P(("wide", "rep"), None)),
        check_vma=False,
    )
```

profile of v0, /device:TPU:1, one launch (start us, length us, event | category | flops | bytes accessed | tf_op | source)
XLA Modules:
  0.0 413.6 jit_solution(4684893846506228546)
XLA Ops:
  8.0 9.0 %reduce-window.19 = s32[32,8,128]{2,1,0:T(8,128)S(1)} reduce-window(s32[32,8,128]{2,1,0:T(8,128)S(1)} %fusion.22, s32[]{:T(128)} %constant.27.clone.1), window={size=1x1x128 pad=0_0x0_0x127_0}, to_apply=%region_8.9 | reduce-window | flops 4161536 | bytes 262148 | tf_op jit(solution)/shard_map/reduce-window.1
  17.5 4.4 %sort.17 = (s32[1024]{0:T(1024)}, s32[1024]{0:T(1024)S(1)}) sort(s32[1024]{0:T(1024)S(1)} %get-tuple-element.53, s32[1024]{0:T(1024)S(1)} %iota.29), dimensions={0}, to_apply=%region_1.2 | sort | flops 10240 | bytes 16384 | tf_op jit(solution)/shard_map/jit(argsort)/sort | solution.py:35
  23.2 12.6 %gather_fusion = s32[3072]{0:T(1024)S(1)} fusion(s32[1024]{0:T(1024)S(1)} %get-tuple-element.30, s32[3072]{0:T(1024)S(1)} %broadcast_clamp_fusion.1), kind=kCustom, calls=%fused_computation | custom fusion | bytes 36864 | tf_op jit(solution)/shard_map/gather | solution.py:39
  35.9 12.6 %gather_fusion.1 = s32[3072]{0:T(1024)S(1)} fusion(s32[1024]{0:T(1024)S(1)} %get-tuple-element.51, s32[3072]{0:T(1024)S(1)} %broadcast_clamp_fusion.2), kind=kCustom, calls=%fused_computation.1 | custom fusion | bytes 36864 | tf_op jit(solution)/shard_map/gather | solution.py:41
  49.3 8.6 %all-to-all-start = ((s32[32,96,1]{1,2,0:T(1,128)}), s32[32,96,1]{1,2,0:T(1,128)S(1)}, u32[]{:S(2)}, u32[]{:S(2)}) async-start(s32[32,96,1]{1,2,0:T(1,128)} %bitcast.6), calls=%async_computation | async-start | bytes 32768 | tf_op jit(solution)/shard_map/all_to_all | solution.py:44
  57.9 5.0 %multiply_reduce_fusion.1 = (f32[1024]{0:T(1024)S(1)}, f32[1024,256]{0,1:T(8,128)S(1)}) fusion(bf16[1024,256]{1,0:T(8,128)(2,1)} %param.10, bf16[1024,1024]{1,0:T(8,128)(2,1)S(1)} %copy-done, bf16[1024,1024]{1,0:T(8,128)(2,1)} %param.9), kind=kOutput, calls=%fused_computation.28 | convolution fusion | flops 2694315008 | bytes 5771264 | tf_op jit(solution)/shard_map/dot_general | solution.py:23
  62.9 1.0 copy-done.2
  64.8 1.2 copy.19
  66.0 13.0 %gather_fusion.2 = bf16[3072,256]{1,0:T(8,128)(2,1)} fusion(bf16[1024,256]{1,0:T(8,128)(2,1)S(1)} %copy.19, s32[3072]{0:T(1024)S(1)} %broadcast_clamp_fusion.2), kind=kCustom, calls=%fused_computation.2 | custom fusion | bytes 3158016 | tf_op jit(solution)/shard_map/gather | solution.py:40
  79.1 2.6 broadcast_select_fusion
  81.7 7.4 %all-to-all-start.1 = ((bf16[32,96,256]{2,1,0:T(8,128)(2,1)}), bf16[32,96,256]{2,1,0:T(8,128)(2,1)}, u32[]{:S(2)}, u32[]{:S(2)}) async-start(bf16[32,96,256]{2,1,0:T(8,128)(2,1)} %broadcast_select_fusion), calls=%async_computation.1 | async-start | bytes 3145728 | tf_op jit(solution)/shard_map/all_to_all | solution.py:43
  90.5 21.3 %all-to-all-done.1 = bf16[32,96,256]{2,1,0:T(8,128)(2,1)} async-done(((bf16[32,96,256]{2,1,0:T(8,128)(2,1)}), bf16[32,96,256]{2,1,0:T(8,128)(2,1)}, u32[]{:S(2)}, u32[]{:S(2)}) %all-to-all-start.1) | async-done | bytes 1572896 | tf_op jit(solution)/shard_map/all_to_all | solution.py:43
  111.8 60.4 %while.10 = (s32[]{:T(128)}, bf16[8,2048,256]{2,1,0:T(8,128)(2,1)}, s32[8]{0:T(128)S(1)}, s32[3072]{0:T(1024)S(1)}, bf16[3072,256]{1,0:T(8,128)(2,1)}, /*index=5*/s32[]{:T(128)}) while((s32[]{:T(128)}, bf16[8,2048,256]{2,1,0:T(8,128)(2,1)}, s32[8]{0:T(128)S(1)}, s32[3072]{0:T(1024)S(1)}, bf16[3072,256]{1,0:T(8,128)(2,1)}, ...), condition=%wide.region_5.6_spmd, body=%wide.region_4.5_spmd.sunk | while | flops 3227518976 | bytes 3698785 | solution.py:55
  113.1 6.3 %fusion.43 = bf16[8,2048,256]{2,1,0:T(8,128)(2,1)} fusion(bf16[8,2048,256]{2,1,0:T(8,128)(2,1)} %get-tuple-element.94, s32[]{:T(128)S(6)} %copy.29, bf16[3072,256]{1,0:T(8,128)(2,1)} %get-tuple-element.103, s32[3072]{0:T(1024)S(1)} %get-tuple-element.102, s32[2048]{0:T(1024)S(1)} %iota_add_fusion.2), kind=kOutput, calls=%fused_computation.10.clone.1 | convolution fusion | flops 3227516928 | bytes 3690500 | tf_op jit(solution)/shard_map/while/body/eval_jaxpr/dot_general | solution.py:52
  120.6 6.4 %fusion.43 = bf16[8,2048,256]{2,1,0:T(8,128)(2,1)} fusion(bf16[8,2048,256]{2,1,0:T(8,128)(2,1)} %get-tuple-element.94, s32[]{:T(128)S(6)} %copy.29, bf16[3072,256]{1,0:T(8,128)(2,1)} %get-tuple-element.103, s32[3072]{0:T(1024)S(1)} %get-tuple-element.102, s32[2048]{0:T(1024)S(1)} %iota_add_fusion.2), kind=kOutput, calls=%fused_computation.10.clone.1 | convolution fusion | flops 3227516928 | bytes 3690500 | tf_op jit(solution)/shard_map/while/body/eval_jaxpr/dot_general | solution.py:52
  128.2 6.3 %fusion.43 = bf16[8,2048,256]{2,1,0:T(8,128)(2,1)} fusion(bf16[8,2048,256]{2,1,0:T(8,128)(2,1)} %get-tuple-element.94, s32[]{:T(128)S(6)} %copy.29, bf16[3072,256]{1,0:T(8,128)(2,1)} %get-tuple-element.103, s32[3072]{0:T(1024)S(1)} %get-tuple-element.102, s32[2048]{0:T(1024)S(1)} %iota_add_fusion.2), kind=kOutput, calls=%fused_computation.10.clone.1 | convolution fusion | flops 3227516928 | bytes 3690500 | tf_op jit(solution)/shard_map/while/body/eval_jaxpr/dot_general | solution.py:52
  135.8 6.3 %fusion.43 = bf16[8,2048,256]{2,1,0:T(8,128)(2,1)} fusion(bf16[8,2048,256]{2,1,0:T(8,128)(2,1)} %get-tuple-element.94, s32[]{:T(128)S(6)} %copy.29, bf16[3072,256]{1,0:T(8,128)(2,1)} %get-tuple-element.103, s32[3072]{0:T(1024)S(1)} %get-tuple-element.102, s32[2048]{0:T(1024)S(1)} %iota_add_fusion.2), kind=kOutput, calls=%fused_computation.10.clone.1 | convolution fusion | flops 3227516928 | bytes 3690500 | tf_op jit(solution)/shard_map/while/body/eval_jaxpr/dot_general | solution.py:52
  143.3 6.3 %fusion.43 = bf16[8,2048,256]{2,1,0:T(8,128)(2,1)} fusion(bf16[8,2048,256]{2,1,0:T(8,128)(2,1)} %get-tuple-element.94, s32[]{:T(128)S(6)} %copy.29, bf16[3072,256]{1,0:T(8,128)(2,1)} %get-tuple-element.103, s32[3072]{0:T(1024)S(1)} %get-tuple-element.102, s32[2048]{0:T(1024)S(1)} %iota_add_fusion.2), kind=kOutput, calls=%fused_computation.10.clone.1 | convolution fusion | flops 3227516928 | bytes 3690500 | tf_op jit(solution)/shard_map/while/body/eval_jaxpr/dot_general | solution.py:52
  150.8 6.3 %fusion.43 = bf16[8,2048,256]{2,1,0:T(8,128)(2,1)} fusion(bf16[8,2048,256]{2,1,0:T(8,128)(2,1)} %get-tuple-element.94, s32[]{:T(128)S(6)} %copy.29, bf16[3072,256]{1,0:T(8,128)(2,1)} %get-tuple-element.103, s32[3072]{0:T(1024)S(1)} %get-tuple-element.102, s32[2048]{0:T(1024)S(1)} %iota_add_fusion.2), kind=kOutput, calls=%fused_computation.10.clone.1 | convolution fusion | flops 3227516928 | bytes 3690500 | tf_op jit(solution)/shard_map/while/body/eval_jaxpr/dot_general | solution.py:52
  158.4 6.3 %fusion.43 = bf16[8,2048,256]{2,1,0:T(8,128)(2,1)} fusion(bf16[8,2048,256]{2,1,0:T(8,128)(2,1)} %get-tuple-element.94, s32[]{:T(128)S(6)} %copy.29, bf16[3072,256]{1,0:T(8,128)(2,1)} %get-tuple-element.103, s32[3072]{0:T(1024)S(1)} %get-tuple-element.102, s32[2048]{0:T(1024)S(1)} %iota_add_fusion.2), kind=kOutput, calls=%fused_computation.10.clone.1 | convolution fusion | flops 3227516928 | bytes 3690500 | tf_op jit(solution)/shard_map/while/body/eval_jaxpr/dot_general | solution.py:52
  165.9 6.3 %fusion.43 = bf16[8,2048,256]{2,1,0:T(8,128)(2,1)} fusion(bf16[8,2048,256]{2,1,0:T(8,128)(2,1)} %get-tuple-element.94, s32[]{:T(128)S(6)} %copy.29, bf16[3072,256]{1,0:T(8,128)(2,1)} %get-tuple-element.103, s32[3072]{0:T(1024)S(1)} %get-tuple-element.102, s32[2048]{0:T(1024)S(1)} %iota_add_fusion.2), kind=kOutput, calls=%fused_computation.10.clone.1 | convolution fusion | flops 3227516928 | bytes 3690500 | tf_op jit(solution)/shard_map/while/body/eval_jaxpr/dot_general | solution.py:52
  172.4 158.7 %all-reduce.2.cloned.1.call-done = bf16[16384,256]{1,0:T(8,128)(2,1)} async-done(((bf16[16384,256]{1,0:T(8,128)(2,1)}), bf16[16384,256]{1,0:T(8,128)(2,1)}) %all-reduce.2.cloned.1.call-update) | async-done | bytes 8388624 | tf_op jit(solution)/shard_map/psum | solution.py:60
  331.1 7.6 %multiply_reduce_fusion = f32[16384]{0:T(1024)S(1)} fusion(bf16[16384,256]{1,0:T(8,128)(2,1)} %all-reduce.2.cloned.1.call-done, bf16[16384,256]{1,0:T(8,128)(2,1)} %param.11), kind=kLoop, calls=%fused_computation.13 | loop fusion | flops 20955136 | bytes 16842752 | tf_op jit(solution)/shard_map/reduce_sum | solution.py:10
  339.4 8.1 %multiply_convert_fusion = bf16[16384,256]{1,0:T(8,128)(2,1)} fusion(bf16[16384,256]{1,0:T(8,128)(2,1)S(1)} %copy-done.1, bf16[16384,256]{1,0:T(8,128)(2,1)} %param.11, f32[16384]{0:T(1024)S(1)} %add_rsqrt_fusion), kind=kLoop, calls=%fused_computation.12 | loop fusion | flops 20971520 | bytes 25231360 | tf_op jit(solution)/shard_map/convert_element_type | solution.py:11
  347.5 16.6 %gather_fusion.3 = bf16[3072,256]{1,0:T(8,128)(2,1)} fusion(bf16[16384,256]{1,0:T(8,128)(2,1)} %multiply_convert_fusion, s32[3072]{0:T(1024)S(1)} %broadcast_clamp_fusion), kind=kCustom, calls=%fused_computation.3 | custom fusion | bytes 3158016 | tf_op jit(solution)/shard_map/gather | solution.py:63
  364.0 7.7 %all-to-all-start.2 = ((bf16[32,96,256]{2,1,0:T(8,128)(2,1)}), bf16[32,96,256]{2,1,0:T(8,128)(2,1)}, u32[]{:S(2)}, u32[]{:S(2)}) async-start(bf16[32,96,256]{2,1,0:T(8,128)(2,1)} %bitcast.41), calls=%async_computation.2 | async-start | bytes 3145728 | tf_op jit(solution)/shard_map/all_to_all | solution.py:64
  371.8 3.1 constant_dynamic-slice_fusion
  374.9 19.6 %all-to-all-done.2 = bf16[32,96,256]{2,1,0:T(8,128)(2,1)} async-done(((bf16[32,96,256]{2,1,0:T(8,128)(2,1)}), bf16[32,96,256]{2,1,0:T(8,128)(2,1)}, u32[]{:S(2)}, u32[]{:S(2)}) %all-to-all-start.2) | async-done | bytes 1572896 | tf_op jit(solution)/shard_map/all_to_all | solution.py:64
  394.5 6.2 %gather_fusion.4 = bf16[1024,256]{1,0:T(8,128)(2,1)} fusion(bf16[3072,256]{1,0:T(8,128)(2,1)} %bitcast.12, s32[1024]{0:T(1024)S(1)} %get-tuple-element.50), kind=kCustom, calls=%fused_computation.4 | custom fusion | bytes 1052672 | tf_op jit(solution)/shard_map/gather | solution.py:65
  400.7 2.0 copy.22
  402.8 2.0 subtract_convert_fusion
  404.8 2.0 copy.23
  (61 shorter events, 16.3 us)
Async XLA Ops:
  7.2 50.8 %copy-start = (bf16[1024,1024]{1,0:T(8,128)(2,1)S(1)}, bf16[1024,1024]{1,0:T(8,128)(2,1)}, u32[]{:S(2)}) copy-start(bf16[1024,1024]{1,0:T(8,128)(2,1)} %param.7) | copy-start | bytes 6291460
  49.3 32.4 %all-to-all-start = ((s32[32,96,1]{1,2,0:T(1,128)}), s32[32,96,1]{1,2,0:T(1,128)S(1)}, u32[]{:S(2)}, u32[]{:S(2)}) async-start(s32[32,96,1]{1,2,0:T(1,128)} %bitcast.6), calls=%async_computation | async-start | bytes 32768 | tf_op jit(solution)/shard_map/all_to_all | solution.py:44
  62.9 1.0 copy-start.2
  81.7 30.2 %all-to-all-start.1 = ((bf16[32,96,256]{2,1,0:T(8,128)(2,1)}), bf16[32,96,256]{2,1,0:T(8,128)(2,1)}, u32[]{:S(2)}, u32[]{:S(2)}) async-start(bf16[32,96,256]{2,1,0:T(8,128)(2,1)} %broadcast_select_fusion), calls=%async_computation.1 | async-start | bytes 3145728 | tf_op jit(solution)/shard_map/all_to_all | solution.py:43
  89.1 242.0 %all-reduce.2.cloned.1.call-start = ((), (), s32[]{:S(2)}) async-start(), calls=%async_computation.3 | async-start | bytes 16777216 | tf_op jit(solution)/shard_map/psum | solution.py:60
  331.1 8.3 %copy-start.1 = (bf16[16384,256]{1,0:T(8,128)(2,1)S(1)}, bf16[16384,256]{1,0:T(8,128)(2,1)}, u32[]{:S(2)}) copy-start(bf16[16384,256]{1,0:T(8,128)(2,1)} %all-reduce.2.cloned.1.call-done) | copy-start | bytes 25165828
  364.0 30.5 %all-to-all-start.2 = ((bf16[32,96,256]{2,1,0:T(8,128)(2,1)}), bf16[32,96,256]{2,1,0:T(8,128)(2,1)}, u32[]{:S(2)}, u32[]{:S(2)}) async-start(bf16[32,96,256]{2,1,0:T(8,128)(2,1)} %bitcast.41), calls=%async_computation.2 | async-start | bytes 3145728 | tf_op jit(solution)/shard_map/all_to_all | solution.py:64
  371.8 31.0 %copy-start.3 = (f32[1024,256]{0,1:T(8,128)S(1)}, f32[1024,256]{0,1:T(8,128)}, u32[]{:S(2)}) copy-start(f32[1024,256]{0,1:T(8,128)} %copy-done.2) | copy-start | bytes 3145732
Sparse Core Ops, SparseCore 0:
  172.4 158.6 all-reduce.1
where the time goes:
time: 415 us; the launch traced here: 414 us
  waiting for transfers between devices  200 us (48%)
  local copies, waits for them, and re-layouts  77 us (19%)
  matrix products  55.5 us (13%)
  other arithmetic  43.2 us (10%)
  starting transfers between devices  24 us (6%)
  between operations  14.3 us (3%)
    psum x1, waiting for transfers between devices, body(): lax.psum(partial_value.astype(jnp.bfloat16), 'rep').astype(jnp.float32)  159 us
    dot_general x8, matrix products, one_block(): return jnp.dot(selector, incoming, preferred_element_type=jnp.float32)  50.5 us
    all_to_all x1, waiting for transfers between devices, body(): lax.all_to_all(outgoing, 'wide', split_axis=0, concat_axis=0, tiled=True)  21.3 us
    all_to_all x1, waiting for transfers between devices, body(): lax.all_to_all(picked, 'wide', split_axis=0, concat_axis=0, tiled=True)  19.6 us
    gather x1, local copies, waits for them, and re-layouts, body(): picked = fresh_table[safe_ids]  16.6 us
    gather x1, local copies, waits for them, and re-layouts, body(): embedded[source]  13 us
    gather x2, local copies, waits for them, and re-layouts, body(): out_ids = jnp.where(valid, local_id[source], -1)  12.7 us
    gather x1, local copies, waits for them, and re-layouts, body(): source = order[position]  12.6 us
  transfers between devices with their start and end apart: 4, of which 3 were waited for; matrix products, arithmetic and copies ran while one was open for 7% of the time, Pallas kernels for 0%

commit v1 on v0

v1 whole, which is shorter than its diff:
```python
import jax
import jax.numpy as jnp
from jax import lax
from jax.sharding import PartitionSpec as P


def normalize(updated):
    return (
        updated * lax.rsqrt(jnp.mean(updated * updated, axis=-1, keepdims=True) + 1e-06)
    ).astype(jnp.bfloat16)


def body(passages, cluster_ids, w_first, w_second, centroids):
    tok_rows = passages.shape[0]
    owners = lax.axis_size("wide")
    replicas = lax.axis_size("rep")
    cent_rows = centroids.shape[0]
    share_rows = cent_rows // replicas
    capacity = 3 * tok_rows // owners
    slots = owners * capacity

    hidden = jax.nn.gelu(
        jnp.dot(passages, w_first, preferred_element_type=jnp.float32), approximate=True
    ).astype(jnp.bfloat16)
    projected = jnp.dot(hidden, w_second, preferred_element_type=jnp.float32)
    embedded = (
        projected * lax.rsqrt(jnp.mean(projected * projected, axis=-1, keepdims=True) + 1e-06)
    ).astype(jnp.bfloat16)

    owner_of = cluster_ids // cent_rows
    local_id = cluster_ids - owner_of * cent_rows
    member = owner_of[:, None] == jnp.arange(owners, dtype=jnp.int32)[None, :]
    row = jnp.arange(tok_rows, dtype=jnp.int32)
    earlier = (row[:, None] > row[None, :]).astype(jnp.bfloat16)
    before = jnp.dot(earlier, member.astype(jnp.bfloat16), preferred_element_type=jnp.float32)
    slot_of = jnp.sum(jnp.where(member, before, 0.0), axis=1).astype(jnp.int32)
    target = owner_of * capacity + slot_of
    place = target[None, :] == jnp.arange(slots, dtype=jnp.int32)[:, None]
    place_bf = place.astype(jnp.bfloat16)
    outgoing = jnp.dot(place_bf, embedded, preferred_element_type=jnp.float32).astype(jnp.bfloat16)
    out_ids = jnp.sum(jnp.where(place, local_id[None, :], 0), axis=1)

    incoming = lax.all_to_all(outgoing, "wide", split_axis=0, concat_axis=0, tiled=True)
    in_ids = lax.all_to_all(out_ids, "wide", split_axis=0, concat_axis=0, tiled=True)

    all_rows = lax.all_gather(incoming, "rep", axis=0, tiled=True)
    all_ids = lax.all_gather(in_ids, "rep", axis=0, tiled=True)

    first_row = lax.axis_index("rep") * share_rows
    queries = jnp.concatenate(
        [first_row + jnp.arange(share_rows, dtype=jnp.int32), in_ids]
    )
    block_rows = 1024
    query_count = queries.shape[0]
    padded = -(-query_count // block_rows) * block_rows
    queries = jnp.pad(queries, (0, padded - query_count), constant_values=-1)

    def one_block(block_ids):
        selector = (block_ids[:, None] == all_ids[None, :]).astype(jnp.bfloat16)
        return jnp.dot(selector, all_rows, preferred_element_type=jnp.float32)

    sums = lax.map(one_block, queries.reshape(-1, block_rows)).reshape(padded, -1)
    share_sum = sums[:share_rows]
    look_sum = sums[share_rows:query_count]

    own_cent = lax.dynamic_slice_in_dim(centroids, first_row, share_rows, 0)
    own_rows = normalize(own_cent.astype(jnp.float32) + share_sum)

    look_cent = centroids[in_ids]
    picked = normalize(look_cent.astype(jnp.float32) + look_sum)
    returned = lax.all_to_all(picked, "wide", split_axis=0, concat_axis=0, tiled=True)
    gathered_rows = jnp.dot(place_bf.T, returned, preferred_element_type=jnp.float32)
    residuals = (embedded.astype(jnp.float32) - gathered_rows).astype(jnp.bfloat16)
    return (own_rows, residuals)


def solution(mesh):
    return jax.shard_map(
        body,
        mesh=mesh,
        in_specs=(P(("wide", "rep"), None), P(("wide", "rep")), P(), P(), P("wide", None)),
        out_specs=(P(("wide", "rep"), None), P(("wide", "rep"), None)),
        check_vma=False,
    )
```

time: 415 us -> 245 us (0.59)
  waiting for transfers between devices: 200 us -> 40.7 us
  local copies, waits for them, and re-layouts: 77 us -> 24.3 us
  blocking collectives: 0 us -> 43.4 us
  matrix products: 55.5 us -> 88.1 us
  other arithmetic: 43.2 us -> 22.3 us
  starting transfers between devices: 24 us -> 11.4 us
    psum x1 -> x0, waiting for transfers between devices: 159 us -> none  [body(): lax.psum(partial_value.astype(jnp.bfloat16), 'rep').astype(jnp.float32)]
    gather x7 -> x1, local copies, waits for them, and re-layouts: 63.2 us -> 16.7 us  [body(): look_cent = centroids[in_ids]]
    dot_general x8 -> x10, matrix products: 50.5 us -> 82.2 us  [the longest x7 73.6 us: one_block(): return jnp.dot(selector, all_rows, preferred_element_type=jnp.float32)]
    all_to_all x0 -> x1, blocking collectives: none -> 31.3 us  [body(): lax.all_to_all(outgoing, 'wide', split_axis=0, concat_axis=0, tiled=True)]
    all_to_all x1 -> x0, waiting for transfers between devices: 21.3 us -> none  [body(): lax.all_to_all(outgoing, 'wide', split_axis=0, concat_axis=0, tiled=True)]
    all_gather x0 -> x1, waiting for transfers between devices: none -> 18.2 us  [body(): all_rows = lax.all_gather(incoming, 'rep', axis=0, tiled=True)]
    all_gather x0 -> x1, blocking collectives: none -> 12.1 us  [body(): all_ids = lax.all_gather(in_ids, 'rep', axis=0, tiled=True)]
    another operation x5 -> x0, other arithmetic: 9.32 us -> none
  transfers between devices with their start and end apart: 4 -> 3, of which waited for: 3 -> 3; matrix products, arithmetic and copies ran while one was open for 7% -> 12% of each run, Pallas kernels for 0% -> 0%
where the time goes in v1:
time: 245 us
  matrix products  88.1 us (36%)
  blocking collectives  43.4 us (18%)
  waiting for transfers between devices  40.7 us (17%)
  local copies, waits for them, and re-layouts  24.3 us (10%)
  other arithmetic  22.3 us (9%)
  between operations  14.2 us (6%)
  starting transfers between devices  11.4 us (5%)
    dot_general x7, matrix products, one_block(): return jnp.dot(selector, all_rows, preferred_element_type=jnp.float32)  73.6 us
    all_to_all x1, blocking collectives, body(): lax.all_to_all(outgoing, 'wide', split_axis=0, concat_axis=0, tiled=True)  31.3 us
    all_gather x1, waiting for transfers between devices, body(): all_rows = lax.all_gather(incoming, 'rep', axis=0, tiled=True)  18.2 us
    gather x1, local copies, waits for them, and re-layouts, body(): look_cent = centroids[in_ids]  16.7 us
    all_to_all x1, waiting for transfers between devices, body(): lax.all_to_all(picked, 'wide', split_axis=0, concat_axis=0, tiled=True)  15.6 us
    all_gather x1, blocking collectives, body(): all_ids = lax.all_gather(in_ids, 'rep', axis=0, tiled=True)  12.1 us
    all_to_all x1, starting transfers between devices, body(): lax.all_to_all(picked, 'wide', split_axis=0, concat_axis=0, tiled=True)  7.76 us
    reduce_sum x2, other arithmetic, normalize(): jnp.mean(updated * updated, axis=-1, keepdims=True) + 1e-06  7.7 us
  transfers between devices with their start and end apart: 3, of which 3 were waited for; matrix products, arithmetic and copies ran while one was open for 12% of the time, Pallas kernels for 0%

profile of v1, /device:TPU:1, one launch (start us, length us, event | category | flops | bytes accessed | tf_op | source)
XLA Modules:
  0.0 244.6 jit_solution(2564046738196507318)
XLA Ops:
  7.2 0.8 add_select_fusion
  8.1 0.5 fusion.29
  8.6 0.7 convert_add_fusion
  9.3 6.0 %multiply_reduce_fusion.2 = (f32[1024]{0:T(1024)S(1)}, f32[1024,256]{0,1:T(8,128)}) fusion(bf16[1024,256]{1,0:T(8,128)(2,1)} %param.10, bf16[1024,1024]{1,0:T(8,128)(2,1)S(1)} %copy-done, bf16[1024,1024]{1,0:T(8,128)(2,1)} %param.9), kind=kOutput, calls=%fused_computation.37 | convolution fusion | flops 2694315008 | bytes 5771264 | tf_op jit(solution)/shard_map/dot_general | solution.py:25
  15.3 3.7 %fusion.23 = bf16[3072,256]{1,0:T(8,128)(2,1)S(1)} fusion(s32[1024]{0:T(1024)S(1)} %get-tuple-element.50, f32[1024,256]{0,1:T(8,128)} %get-tuple-element.53, f32[1024]{0:T(1024)S(1)} %add_rsqrt_fusion.2), kind=kOutput, calls=%fused_computation.28 | convolution fusion | flops 1615069184 | bytes 2629632 | tf_op jit(solution)/shard_map/dot_general | solution.py:40
  19.0 31.3 %all_to_all.36 = bf16[32,96,256]{2,1,0:T(8,128)(2,1)} all-to-all(bf16[32,96,256]{2,1,0:T(8,128)(2,1)S(1)} %bitcast.36), channel_id=1, replica_groups=mesh['wide'=32,'rep'=4] {'wide'}, dimensions={0} | all-to-all | bytes 3145728 | tf_op jit(solution)/shard_map/all_to_all | solution.py:43
  50.3 1.3 select_reduce_fusion
  51.7 0.7 all_to_all.24
  52.4 3.6 %all-to-all-start = ((s32[32,96,1]{1,2,0:T(1,128)}), s32[32,96,1]{1,2,0:T(1,128)S(1)}, u32[]{:S(2)}, u32[]{:S(2)}) async-start(s32[32,96,1]{1,2,0:T(1,128)} %bitcast.2), calls=%async_computation | async-start | bytes 32768 | tf_op jit(solution)/shard_map/all_to_all | solution.py:44
  56.0 6.9 %all-to-all-done = s32[32,96,1]{1,2,0:T(1,128)S(1)} async-done(((s32[32,96,1]{1,2,0:T(1,128)}), s32[32,96,1]{1,2,0:T(1,128)S(1)}, u32[]{:S(2)}, u32[]{:S(2)}) %all-to-all-start) | async-done | bytes 12320 | tf_op jit(solution)/shard_map/all_to_all | solution.py:44
  63.4 0.7 reduce.6
  64.3 16.7 %gather_fusion = bf16[3072,256]{1,0:T(8,128)(2,1)} fusion(bf16[16384,256]{1,0:T(8,128)(2,1)} %param.11, s32[3072]{0:T(1024)S(1)} %broadcast_clamp_fusion), kind=kCustom, calls=%fused_computation | custom fusion | bytes 3158016 | tf_op jit(solution)/shard_map/gather | solution.py:69
  81.0 3.4 %convert_element_type.58 = f32[3072,256]{1,0:T(8,128)} convert(bf16[3072,256]{1,0:T(8,128)(2,1)} %gather_fusion) | non-fusion elementwise | flops 786432 | bytes 4718592 | tf_op jit(solution)/shard_map/convert_element_type | solution.py:70
  84.4 12.1 %all_gather.6 = s32[12288]{0:T(1024)S(1)} all-gather(s32[3072]{0:T(1024)S(1)} %all_to_all.26), channel_id=1, replica_groups=mesh['wide'=32,'rep'=4] {'rep'}, dimensions={0}, use_global_device_ids=true | all-gather | bytes 61440 | tf_op jit(solution)/shard_map/all_gather | solution.py:47
  96.6 18.2 %all-gather.2.cloned.1.call-done = bf16[12288,256]{1,0:T(8,128)(2,1)} async-done(((bf16[3072,256]{1,0:T(8,128)(2,1)}), bf16[12288,256]{1,0:T(8,128)(2,1)}) %all-gather.2.cloned.1.call-update) | async-done | bytes 6291472 | tf_op jit(solution)/shard_map/all_gather | solution.py:46
  114.8 73.7 %while.10 = (s32[]{:T(128)}, f32[7,1024,256]{2,1,0:T(8,128)}, s32[7,1024]{1,0:T(8,128)S(1)}, s32[12288]{0:T(1024)S(1)}, bf16[12288,256]{1,0:T(8,128)(2,1)}, /*index=5*/s32[]{:T(128)}) while((s32[]{:T(128)}, f32[7,1024,256]{2,1,0:T(8,128)}, s32[7,1024]{1,0:T(8,128)S(1)}, s32[12288]{0:T(1024)S(1)}, bf16[12288,256]{1,0:T(8,128)(2,1)}, ...), condition=%wide.region_4.5_spmd, body=%wide.region_3.4_spmd.sunk | while | flops 6455033856 | bytes 7402057 | solution.py:62
  114.8 10.6 %fusion.49 = f32[7,1024,256]{2,1,0:T(8,128)} fusion(f32[7,1024,256]{2,1,0:T(8,128)} %get-tuple-element.92, s32[]{:T(128)} %get-tuple-element.91, bf16[12288,256]{1,0:T(8,128)(2,1)} %get-tuple-element.101, s32[12288]{0:T(1024)S(1)} %get-tuple-element.100, s32[1024]{0:T(1024)S(1)} %bitcast.38), kind=kOutput, calls=%fused_computation.6.clone.1 | convolution fusion | flops 6455033856 | bytes 7393792 | tf_op jit(solution)/shard_map/while/body/eval_jaxpr/dot_general | solution.py:60
  125.4 10.5 %fusion.49 = f32[7,1024,256]{2,1,0:T(8,128)} fusion(f32[7,1024,256]{2,1,0:T(8,128)} %get-tuple-element.92, s32[]{:T(128)} %get-tuple-element.91, bf16[12288,256]{1,0:T(8,128)(2,1)} %get-tuple-element.101, s32[12288]{0:T(1024)S(1)} %get-tuple-element.100, s32[1024]{0:T(1024)S(1)} %bitcast.38), kind=kOutput, calls=%fused_computation.6.clone.1 | convolution fusion | flops 6455033856 | bytes 7393792 | tf_op jit(solution)/shard_map/while/body/eval_jaxpr/dot_general | solution.py:60
  135.9 10.5 %fusion.49 = f32[7,1024,256]{2,1,0:T(8,128)} fusion(f32[7,1024,256]{2,1,0:T(8,128)} %get-tuple-element.92, s32[]{:T(128)} %get-tuple-element.91, bf16[12288,256]{1,0:T(8,128)(2,1)} %get-tuple-element.101, s32[12288]{0:T(1024)S(1)} %get-tuple-element.100, s32[1024]{0:T(1024)S(1)} %bitcast.38), kind=kOutput, calls=%fused_computation.6.clone.1 | convolution fusion | flops 6455033856 | bytes 7393792 | tf_op jit(solution)/shard_map/while/body/eval_jaxpr/dot_general | solution.py:60
  146.4 10.5 %fusion.49 = f32[7,1024,256]{2,1,0:T(8,128)} fusion(f32[7,1024,256]{2,1,0:T(8,128)} %get-tuple-element.92, s32[]{:T(128)} %get-tuple-element.91, bf16[12288,256]{1,0:T(8,128)(2,1)} %get-tuple-element.101, s32[12288]{0:T(1024)S(1)} %get-tuple-element.100, s32[1024]{0:T(1024)S(1)} %bitcast.38), kind=kOutput, calls=%fused_computation.6.clone.1 | convolution fusion | flops 6455033856 | bytes 7393792 | tf_op jit(solution)/shard_map/while/body/eval_jaxpr/dot_general | solution.py:60
  156.9 10.5 %fusion.49 = f32[7,1024,256]{2,1,0:T(8,128)} fusion(f32[7,1024,256]{2,1,0:T(8,128)} %get-tuple-element.92, s32[]{:T(128)} %get-tuple-element.91, bf16[12288,256]{1,0:T(8,128)(2,1)} %get-tuple-element.101, s32[12288]{0:T(1024)S(1)} %get-tuple-element.100, s32[1024]{0:T(1024)S(1)} %bitcast.38), kind=kOutput, calls=%fused_computation.6.clone.1 | convolution fusion | flops 6455033856 | bytes 7393792 | tf_op jit(solution)/shard_map/while/body/eval_jaxpr/dot_general | solution.py:60
  167.5 10.5 %fusion.49 = f32[7,1024,256]{2,1,0:T(8,128)} fusion(f32[7,1024,256]{2,1,0:T(8,128)} %get-tuple-element.92, s32[]{:T(128)} %get-tuple-element.91, bf16[12288,256]{1,0:T(8,128)(2,1)} %get-tuple-element.101, s32[12288]{0:T(1024)S(1)} %get-tuple-element.100, s32[1024]{0:T(1024)S(1)} %bitcast.38), kind=kOutput, calls=%fused_computation.6.clone.1 | convolution fusion | flops 6455033856 | bytes 7393792 | tf_op jit(solution)/shard_map/while/body/eval_jaxpr/dot_general | solution.py:60
  178.0 10.5 %fusion.49 = f32[7,1024,256]{2,1,0:T(8,128)} fusion(f32[7,1024,256]{2,1,0:T(8,128)} %get-tuple-element.92, s32[]{:T(128)} %get-tuple-element.91, bf16[12288,256]{1,0:T(8,128)(2,1)} %get-tuple-element.101, s32[12288]{0:T(1024)S(1)} %get-tuple-element.100, s32[1024]{0:T(1024)S(1)} %bitcast.38), kind=kOutput, calls=%fused_computation.6.clone.1 | convolution fusion | flops 6455033856 | bytes 7393792 | tf_op jit(solution)/shard_map/while/body/eval_jaxpr/dot_general | solution.py:60
  188.5 4.8 %slice.12 = f32[4,1024,256]{2,1,0:T(8,128)} slice(f32[7,1024,256]{2,1,0:T(8,128)} %get-tuple-element.29), slice={[0:4], [0:1024], [0:256]} | slice | bytes 8388608 | tf_op jit(solution)/shard_map/slice | solution.py:63
  193.3 4.1 %multiply_reduce_fusion.1 = (f32[3,1024]{1,0:T(4,128)S(1)}, f32[3,1024,256]{2,1,0:T(8,128)}) fusion(f32[3,1024,256]{2,1,0:T(8,128)S(1)} %bitcast.33, f32[7,1024,256]{2,1,0:T(8,128)} %get-tuple-element.29), kind=kLoop, calls=%fused_computation.30 | loop fusion | flops 2356224 | bytes 9449472 | tf_op jit(solution)/shard_map/reduce_sum | solution.py:9
  197.4 4.5 %multiply_convert_fusion.1 = bf16[32,96,256]{2,1,0:T(8,128)(2,1)} fusion(f32[32,96,256]{2,1,0:T(8,128)} %bitcast.32, f32[32,96,256]{2,1,0:T(8,128)} %bitcast.34, f32[32,96]{1,0:T(8,128)S(1)} %rsqrt.30), kind=kLoop, calls=%fused_computation.29 | loop fusion | flops 2359296 | bytes 7876608 | tf_op jit(solution)/shard_map/convert_element_type | solution.py:10
  202.0 7.8 %all-to-all-start.2 = ((bf16[32,96,256]{2,1,0:T(8,128)(2,1)}), bf16[32,96,256]{2,1,0:T(8,128)(2,1)}, u32[]{:S(2)}, u32[]{:S(2)}) async-start(bf16[32,96,256]{2,1,0:T(8,128)(2,1)} %multiply_convert_fusion.1), calls=%async_computation.2 | async-start | bytes 3145728 | tf_op jit(solution)/shard_map/all_to_all | solution.py:71
  209.8 3.6 %multiply_reduce_fusion = f32[4096]{0:T(1024)S(1)} fusion(f32[4,1024,256]{2,1,0:T(8,128)} %slice.12, bf16[16384,256]{1,0:T(8,128)(2,1)} %param.11, s32[]{:T(128)S(6)} %select_n.26), kind=kLoop, calls=%fused_computation.25 | loop fusion | flops 4190208 | bytes 6307844 | tf_op jit(solution)/shard_map/reduce_sum | solution.py:9
  213.8 3.0 %multiply_convert_fusion = bf16[4096,256]{1,0:T(8,128)(2,1)} fusion(f32[4,1024,256]{2,1,0:T(8,128)S(1)} %copy-done.1, f32[4096]{0:T(1024)S(1)} %add_rsqrt_fusion.1, bf16[16384,256]{1,0:T(8,128)(2,1)} %param.11, s32[]{:T(128)S(6)} %select_n.26), kind=kLoop, calls=%fused_computation.24 | loop fusion | flops 4194304 | bytes 8404996 | tf_op jit(solution)/shard_map/convert_element_type | solution.py:10
  216.8 15.6 %all-to-all-done.2 = bf16[32,96,256]{2,1,0:T(8,128)(2,1)} async-done(((bf16[32,96,256]{2,1,0:T(8,128)(2,1)}), bf16[32,96,256]{2,1,0:T(8,128)(2,1)}, u32[]{:S(2)}, u32[]{:S(2)}) %all-to-all-start.2) | async-done | bytes 1572896 | tf_op jit(solution)/shard_map/all_to_all | solution.py:71
  232.4 4.3 %fusion.27 = bf16[1024,256]{0,1:T(8,128)(2,1)S(1)} fusion(bf16[3072,256]{1,0:T(8,128)(2,1)} %bitcast.10, s32[1024]{0:T(1024)S(1)} %get-tuple-element.50, f32[1024,256]{0,1:T(8,128)} %get-tuple-element.53, f32[1024]{0:T(1024)S(1)} %add_rsqrt_fusion.2), kind=kOutput, calls=%fused_computation.33 | convolution fusion | flops 1615069184 | bytes 3153920 | tf_op jit(solution)/shard_map/dot_general | solution.py:72
  236.7 1.0 copy.16
  (28 shorter events, 1.3 us)
Async XLA Ops:
  7.2 2.1 copy-start
  7.2 107.6 %all-gather.2.cloned.1.call-start = ((), (), s32[]{:S(2)}) async-start(), calls=%async_computation.3 | async-start | bytes 7864320 | tf_op jit(solution)/shard_map/all_gather | solution.py:46
  52.4 10.5 %all-to-all-start = ((s32[32,96,1]{1,2,0:T(1,128)}), s32[32,96,1]{1,2,0:T(1,128)S(1)}, u32[]{:S(2)}, u32[]{:S(2)}) async-start(s32[32,96,1]{1,2,0:T(1,128)} %bitcast.2), calls=%async_computation | async-start | bytes 32768 | tf_op jit(solution)/shard_map/all_to_all | solution.py:44
  188.5 4.8 %copy-start.2 = (f32[3072,256]{1,0:T(8,128)S(1)}, f32[3072,256]{1,0:T(8,128)}, u32[]{:S(2)}) copy-start(f32[3072,256]{1,0:T(8,128)} %convert_element_type.58) | copy-start | bytes 9437188
  202.0 30.5 %all-to-all-start.2 = ((bf16[32,96,256]{2,1,0:T(8,128)(2,1)}), bf16[32,96,256]{2,1,0:T(8,128)(2,1)}, u32[]{:S(2)}, u32[]{:S(2)}) async-start(bf16[32,96,256]{2,1,0:T(8,128)(2,1)} %multiply_convert_fusion.1), calls=%async_computation.2 | async-start | bytes 3145728 | tf_op jit(solution)/shard_map/all_to_all | solution.py:71
  209.7 4.1 %copy-start.1 = (f32[4,1024,256]{2,1,0:T(8,128)S(1)}, f32[4,1024,256]{2,1,0:T(8,128)}, u32[]{:S(2)}) copy-start(f32[4,1024,256]{2,1,0:T(8,128)} %slice.12) | copy-start | bytes 12582916
Sparse Core Ops, SparseCore 0:
  50.4 64.3 all-gather.1

commit v2 on v1

--- a/solution.py
+++ b/solution.py
@@ -19,14 +19,6 @@
     capacity = 3 * tok_rows // owners
     slots = owners * capacity
 
-    hidden = jax.nn.gelu(
-        jnp.dot(passages, w_first, preferred_element_type=jnp.float32), approximate=True
-    ).astype(jnp.bfloat16)
-    projected = jnp.dot(hidden, w_second, preferred_element_type=jnp.float32)
-    embedded = (
-        projected * lax.rsqrt(jnp.mean(projected * projected, axis=-1, keepdims=True) + 1e-06)
-    ).astype(jnp.bfloat16)
-
     owner_of = cluster_ids // cent_rows
     local_id = cluster_ids - owner_of * cent_rows
     member = owner_of[:, None] == jnp.arange(owners, dtype=jnp.int32)[None, :]
@@ -37,16 +29,36 @@
     target = owner_of * capacity + slot_of
     place = target[None, :] == jnp.arange(slots, dtype=jnp.int32)[:, None]
     place_bf = place.astype(jnp.bfloat16)
-    outgoing = jnp.dot(place_bf, embedded, preferred_element_type=jnp.float32).astype(jnp.bfloat16)
     out_ids = jnp.sum(jnp.where(place, local_id[None, :], 0), axis=1)
 
-    incoming = lax.all_to_all(outgoing, "wide", split_axis=0, concat_axis=0, tiled=True)
-    in_ids = lax.all_to_all(out_ids, "wide", split_axis=0, concat_axis=0, tiled=True)
+    both = ("wide", "rep")
+    ids_out = jnp.broadcast_to(out_ids.reshape(owners, 1, capacity), (owners, replicas, capacity))
+    all_ids = lax.all_to_all(
+        ids_out.reshape(-1), both, split_axis=0, concat_axis=0, tiled=True
+    )
+    my_rep = lax.axis_index("rep")
+    in_ids = lax.dynamic_index_in_dim(
+        all_ids.reshape(owners, replicas, capacity), my_rep, axis=1, keepdims=False
+    ).reshape(slots)
 
-    all_rows = lax.all_gather(incoming, "rep", axis=0, tiled=True)
-    all_ids = lax.all_gather(in_ids, "rep", axis=0, tiled=True)
+    hidden = jax.nn.gelu(
+        jnp.dot(passages, w_first, preferred_element_type=jnp.float32), approximate=True
+    ).astype(jnp.bfloat16)
+    projected = jnp.dot(hidden, w_second, preferred_element_type=jnp.float32)
+    embedded = (
+        projected * lax.rsqrt(jnp.mean(projected * projected, axis=-1, keepdims=True) + 1e-06)
+    ).astype(jnp.bfloat16)
+    emb_width = embedded.shape[1]
 
-    first_row = lax.axis_index("rep") * share_rows
+    outgoing = jnp.dot(place_bf, embedded, preferred_element_type=jnp.float32).astype(jnp.bfloat16)
+    rows_out = jnp.broadcast_to(
+        outgoing.reshape(owners, 1, capacity, emb_width), (owners, replicas, capacity, emb_width)
+    )
+    all_rows = lax.all_to_all(
+        rows_out.reshape(-1, emb_width), both, split_axis=0, concat_axis=0, tiled=True
+    )
+
+    first_row = my_rep * share_rows
     queries = jnp.concatenate(
         [first_row + jnp.arange(share_rows, dtype=jnp.int32), in_ids]
     )

time: 245 us -> 244 us (level)
  blocking collectives: 43.4 us -> 0 us
  waiting for transfers between devices: 40.7 us -> 69.6 us
  starting transfers between devices: 11.4 us -> 31.2 us
  between operations: 14.2 us -> 0.79 us
  local copies, waits for them, and re-layouts: 24.3 us -> 30 us
    all_to_all x1 -> x2, waiting for transfers between devices: 6.86 us -> 54 us  [the longest x1 54 us: body(): lax.all_to_all(rows_out.reshape(-1, emb_width), both, split_axis=0, conca...]
    all_to_all x1 -> x0, blocking collectives: 31.3 us -> none  [body(): lax.all_to_all(outgoing, 'wide', split_axis=0, concat_axis=0, tiled=True)]
    all_gather x1 -> x0, waiting for transfers between devices: 18.2 us -> none  [body(): all_rows = lax.all_gather(incoming, 'rep', axis=0, tiled=True)]
    all_to_all x1 -> x2, starting transfers between devices: 3.63 us -> 21.7 us  [the longest x1 11.5 us: body(): lax.all_to_all(ids_out.reshape(-1), both, split_axis=0, concat_axis=0, ti...]
    all_gather x1 -> x0, blocking collectives: 12.1 us -> none  [body(): all_ids = lax.all_gather(in_ids, 'rep', axis=0, tiled=True)]
    broadcast_in_dim x0 -> x3, local copies, waits for them, and re-layouts: none -> 5.53 us  [the longest x1 4.81 us: body(): jnp.broadcast_to(outgoing.reshape(owners, 1, capacity, emb_width), (owner...]
  transfers between devices with their start and end apart: 3 -> 3, of which waited for: 3 -> 2; matrix products, arithmetic and copies ran while one was open for 12% -> 16% of each run, Pallas kernels for 0% -> 0%
where the time goes in v2:
time: 244 us; the launch traced here: 243 us
  matrix products  89.2 us (37%)
  waiting for transfers between devices  69.6 us (29%)
  starting transfers between devices  31.2 us (13%)
  local copies, waits for them, and re-layouts  30 us (12%)
  other arithmetic  22.5 us (9%)
    dot_general x7, matrix products, one_block(): return jnp.dot(selector, all_rows, preferred_element_type=jnp.float32)  73.5 us
    all_to_all x1, waiting for transfers between devices, body(): lax.all_to_all(rows_out.reshape(-1, emb_width), both, split_axis=0, conca...  54 us
    gather x1, local copies, waits for them, and re-layouts, body(): look_cent = centroids[in_ids]  16.7 us
    all_to_all x1, waiting for transfers between devices, body(): lax.all_to_all(picked, 'wide', split_axis=0, concat_axis=0, tiled=True)  15.6 us
    all_to_all x1, starting transfers between devices, body(): lax.all_to_all(ids_out.reshape(-1), both, split_axis=0, concat_axis=0, ti...  11.5 us
    all_to_all x1, starting transfers between devices, body(): lax.all_to_all(rows_out.reshape(-1, emb_width), both, split_axis=0, conca...  10.2 us
    all_to_all x1, starting transfers between devices, body(): lax.all_to_all(picked, 'wide', split_axis=0, concat_axis=0, tiled=True)  9.51 us
    reduce_sum x2, other arithmetic, normalize(): jnp.mean(updated * updated, axis=-1, keepdims=True) + 1e-06  7.78 us
  transfers between devices with their start and end apart: 3, of which 2 were waited for; matrix products, arithmetic and copies ran while one was open for 16% of the time, Pallas kernels for 0%

profile of v2, /device:TPU:1, one launch (start us, length us, event | category | flops | bytes accessed | tf_op | source)
XLA Modules:
  0.0 243.2 jit_solution(16094324697574655988)
XLA Ops:
  0.6 0.8 add_select_fusion
  1.5 0.5 fusion.29
  2.0 0.7 convert_add_fusion
  2.7 1.4 select_reduce_fusion
  4.2 0.6 broadcast_in_dim.55
  4.8 11.5 %all-to-all-start = ((s32[128,96,1]{1,2,0:T(1,128)}), s32[128,96,1]{1,2,0:T(1,128)S(1)}, u32[]{:S(2)}, u32[]{:S(2)}) async-start(s32[128,96,1]{1,2,0:T(1,128)} %bitcast.2), calls=%async_computation | async-start | bytes 131072 | tf_op jit(solution)/shard_map/all_to_all | solution.py:36
  16.3 6.0 %multiply_reduce_fusion.2 = (f32[1024]{0:T(1024)S(1)}, f32[1024,256]{0,1:T(8,128)}) fusion(bf16[1024,256]{1,0:T(8,128)(2,1)} %param.10, bf16[1024,1024]{1,0:T(8,128)(2,1)S(1)} %copy-done, bf16[1024,1024]{1,0:T(8,128)(2,1)} %param.9), kind=kOutput, calls=%fused_computation.37 | convolution fusion | flops 2694315008 | bytes 5771264 | tf_op jit(solution)/shard_map/dot_general | solution.py:47
  22.3 4.8 %fusion.23 = bf16[3072,256]{1,0:T(8,128)(2,1)} fusion(s32[1024]{0:T(1024)S(1)} %get-tuple-element.52, f32[1024,256]{0,1:T(8,128)} %get-tuple-element.55, f32[1024]{0:T(1024)S(1)} %add_rsqrt_fusion.2), kind=kOutput, calls=%fused_computation.28 | convolution fusion | flops 1615069184 | bytes 2629632 | tf_op jit(solution)/shard_map/dot_general | solution.py:53
  27.1 4.8 %broadcast_in_dim.57 = bf16[32,4,96,256]{3,2,1,0:T(8,128)(2,1)} broadcast(bf16[32,96,256]{2,1,0:T(8,128)(2,1)} %bitcast.38), dimensions={0,2,3} | broadcast | bytes 7864320 | tf_op jit(solution)/shard_map/broadcast_in_dim | solution.py:54
  31.9 10.2 %all-to-all-start.1 = ((bf16[128,96,256]{2,1,0:T(8,128)(2,1)}), bf16[128,96,256]{2,1,0:T(8,128)(2,1)}, u32[]{:S(2)}, u32[]{:S(2)}) async-start(bf16[128,96,256]{2,1,0:T(8,128)(2,1)} %bitcast.36), calls=%async_computation.1 | async-start | bytes 12582912 | tf_op jit(solution)/shard_map/all_to_all | solution.py:57
  42.7 0.7 fusion.37
  43.5 0.8 reduce.10
  44.5 16.7 %gather_fusion = bf16[3072,256]{1,0:T(8,128)(2,1)} fusion(bf16[16384,256]{1,0:T(8,128)(2,1)} %param.11, s32[3072]{0:T(1024)S(1)} %broadcast_clamp_fusion), kind=kCustom, calls=%fused_computation | custom fusion | bytes 3158016 | tf_op jit(solution)/shard_map/gather | solution.py:81
  61.2 3.4 %convert_element_type.58 = f32[3072,256]{1,0:T(8,128)} convert(bf16[3072,256]{1,0:T(8,128)(2,1)} %gather_fusion) | non-fusion elementwise | flops 786432 | bytes 4718592 | tf_op jit(solution)/shard_map/convert_element_type | solution.py:82
  64.5 54.0 %all-to-all-done.1 = bf16[128,96,256]{2,1,0:T(8,128)(2,1)} async-done(((bf16[128,96,256]{2,1,0:T(8,128)(2,1)}), bf16[128,96,256]{2,1,0:T(8,128)(2,1)}, u32[]{:S(2)}, u32[]{:S(2)}) %all-to-all-start.1) | async-done | bytes 6291488 | tf_op jit(solution)/shard_map/all_to_all | solution.py:57
  118.5 73.6 %while.10 = (s32[]{:T(128)}, f32[7,1024,256]{2,1,0:T(8,128)}, s32[7,1024]{1,0:T(8,128)S(1)}, s32[12288]{0:T(1024)S(1)}, bf16[12288,256]{1,0:T(8,128)(2,1)}, /*index=5*/s32[]{:T(128)}) while((s32[]{:T(128)}, f32[7,1024,256]{2,1,0:T(8,128)}, s32[7,1024]{1,0:T(8,128)S(1)}, s32[12288]{0:T(1024)S(1)}, bf16[12288,256]{1,0:T(8,128)(2,1)}, ...), condition=%wide.region_4.5_spmd, body=%wide.region_3.4_spmd.sunk | while | flops 6455033856 | bytes 7402057 | solution.py:74
  118.5 10.5 %fusion.50 = f32[7,1024,256]{2,1,0:T(8,128)} fusion(f32[7,1024,256]{2,1,0:T(8,128)} %get-tuple-element.94, s32[]{:T(128)} %get-tuple-element.93, bf16[12288,256]{1,0:T(8,128)(2,1)} %get-tuple-element.103, s32[12288]{0:T(1024)S(1)} %get-tuple-element.102, s32[1024]{0:T(1024)S(1)} %bitcast.40), kind=kOutput, calls=%fused_computation.6.clone.1 | convolution fusion | flops 6455033856 | bytes 7393792 | tf_op jit(solution)/shard_map/while/body/eval_jaxpr/dot_general | solution.py:72
  129.0 10.5 %fusion.50 = f32[7,1024,256]{2,1,0:T(8,128)} fusion(f32[7,1024,256]{2,1,0:T(8,128)} %get-tuple-element.94, s32[]{:T(128)} %get-tuple-element.93, bf16[12288,256]{1,0:T(8,128)(2,1)} %get-tuple-element.103, s32[12288]{0:T(1024)S(1)} %get-tuple-element.102, s32[1024]{0:T(1024)S(1)} %bitcast.40), kind=kOutput, calls=%fused_computation.6.clone.1 | convolution fusion | flops 6455033856 | bytes 7393792 | tf_op jit(solution)/shard_map/while/body/eval_jaxpr/dot_general | solution.py:72
  139.6 10.5 %fusion.50 = f32[7,1024,256]{2,1,0:T(8,128)} fusion(f32[7,1024,256]{2,1,0:T(8,128)} %get-tuple-element.94, s32[]{:T(128)} %get-tuple-element.93, bf16[12288,256]{1,0:T(8,128)(2,1)} %get-tuple-element.103, s32[12288]{0:T(1024)S(1)} %get-tuple-element.102, s32[1024]{0:T(1024)S(1)} %bitcast.40), kind=kOutput, calls=%fused_computation.6.clone.1 | convolution fusion | flops 6455033856 | bytes 7393792 | tf_op jit(solution)/shard_map/while/body/eval_jaxpr/dot_general | solution.py:72
  150.1 10.5 %fusion.50 = f32[7,1024,256]{2,1,0:T(8,128)} fusion(f32[7,1024,256]{2,1,0:T(8,128)} %get-tuple-element.94, s32[]{:T(128)} %get-tuple-element.93, bf16[12288,256]{1,0:T(8,128)(2,1)} %get-tuple-element.103, s32[12288]{0:T(1024)S(1)} %get-tuple-element.102, s32[1024]{0:T(1024)S(1)} %bitcast.40), kind=kOutput, calls=%fused_computation.6.clone.1 | convolution fusion | flops 6455033856 | bytes 7393792 | tf_op jit(solution)/shard_map/while/body/eval_jaxpr/dot_general | solution.py:72
  160.6 10.5 %fusion.50 = f32[7,1024,256]{2,1,0:T(8,128)} fusion(f32[7,1024,256]{2,1,0:T(8,128)} %get-tuple-element.94, s32[]{:T(128)} %get-tuple-element.93, bf16[12288,256]{1,0:T(8,128)(2,1)} %get-tuple-element.103, s32[12288]{0:T(1024)S(1)} %get-tuple-element.102, s32[1024]{0:T(1024)S(1)} %bitcast.40), kind=kOutput, calls=%fused_computation.6.clone.1 | convolution fusion | flops 6455033856 | bytes 7393792 | tf_op jit(solution)/shard_map/while/body/eval_jaxpr/dot_general | solution.py:72
  171.1 10.5 %fusion.50 = f32[7,1024,256]{2,1,0:T(8,128)} fusion(f32[7,1024,256]{2,1,0:T(8,128)} %get-tuple-element.94, s32[]{:T(128)} %get-tuple-element.93, bf16[12288,256]{1,0:T(8,128)(2,1)} %get-tuple-element.103, s32[12288]{0:T(1024)S(1)} %get-tuple-element.102, s32[1024]{0:T(1024)S(1)} %bitcast.40), kind=kOutput, calls=%fused_computation.6.clone.1 | convolution fusion | flops 6455033856 | bytes 7393792 | tf_op jit(solution)/shard_map/while/body/eval_jaxpr/dot_general | solution.py:72
  181.6 10.5 %fusion.50 = f32[7,1024,256]{2,1,0:T(8,128)} fusion(f32[7,1024,256]{2,1,0:T(8,128)} %get-tuple-element.94, s32[]{:T(128)} %get-tuple-element.93, bf16[12288,256]{1,0:T(8,128)(2,1)} %get-tuple-element.103, s32[12288]{0:T(1024)S(1)} %get-tuple-element.102, s32[1024]{0:T(1024)S(1)} %bitcast.40), kind=kOutput, calls=%fused_computation.6.clone.1 | convolution fusion | flops 6455033856 | bytes 7393792 | tf_op jit(solution)/shard_map/while/body/eval_jaxpr/dot_general | solution.py:72
  192.2 4.8 %slice.12 = f32[4,1024,256]{2,1,0:T(8,128)} slice(f32[7,1024,256]{2,1,0:T(8,128)} %get-tuple-element.29), slice={[0:4], [0:1024], [0:256]} | slice | bytes 8388608 | tf_op jit(solution)/shard_map/slice | solution.py:75
  197.0 4.1 %multiply_reduce_fusion.1 = (f32[3,1024]{1,0:T(4,128)S(1)}, f32[3,1024,256]{2,1,0:T(8,128)}) fusion(f32[3,1024,256]{2,1,0:T(8,128)S(1)} %bitcast.35, f32[7,1024,256]{2,1,0:T(8,128)} %get-tuple-element.29), kind=kLoop, calls=%fused_computation.30 | loop fusion | flops 2356224 | bytes 9449472 | tf_op jit(solution)/shard_map/reduce_sum | solution.py:9
  201.2 4.5 %multiply_convert_fusion.1 = bf16[32,96,256]{2,1,0:T(8,128)(2,1)} fusion(f32[32,96,256]{2,1,0:T(8,128)} %bitcast.34, f32[32,96,256]{2,1,0:T(8,128)} %bitcast.37, f32[32,96]{1,0:T(8,128)S(1)} %rsqrt.30), kind=kLoop, calls=%fused_computation.29 | loop fusion | flops 2359296 | bytes 7876608 | tf_op jit(solution)/shard_map/convert_element_type | solution.py:10
  205.7 9.5 %all-to-all-start.2 = ((bf16[32,96,256]{2,1,0:T(8,128)(2,1)}), bf16[32,96,256]{2,1,0:T(8,128)(2,1)}, u32[]{:S(2)}, u32[]{:S(2)}) async-start(bf16[32,96,256]{2,1,0:T(8,128)(2,1)} %multiply_convert_fusion.1), calls=%async_computation.2 | async-start | bytes 3145728 | tf_op jit(solution)/shard_map/all_to_all | solution.py:83
  215.3 3.6 %multiply_reduce_fusion = f32[4096]{0:T(1024)S(1)} fusion(f32[4,1024,256]{2,1,0:T(8,128)} %slice.12, bf16[16384,256]{1,0:T(8,128)(2,1)} %param.11, s32[]{:T(128)S(6)} %select_n.30), kind=kLoop, calls=%fused_computation.25 | loop fusion | flops 4190208 | bytes 6307844 | tf_op jit(solution)/shard_map/reduce_sum | solution.py:9
  219.3 3.0 %multiply_convert_fusion = bf16[4096,256]{1,0:T(8,128)(2,1)} fusion(f32[4,1024,256]{2,1,0:T(8,128)S(1)} %copy-done.1, f32[4096]{0:T(1024)S(1)} %add_rsqrt_fusion.1, bf16[16384,256]{1,0:T(8,128)(2,1)} %param.11, s32[]{:T(128)S(6)} %select_n.30), kind=kLoop, calls=%fused_computation.24 | loop fusion | flops 4194304 | bytes 8404996 | tf_op jit(solution)/shard_map/convert_element_type | solution.py:10
  222.3 15.6 %all-to-all-done.2 = bf16[32,96,256]{2,1,0:T(8,128)(2,1)} async-done(((bf16[32,96,256]{2,1,0:T(8,128)(2,1)}), bf16[32,96,256]{2,1,0:T(8,128)(2,1)}, u32[]{:S(2)}, u32[]{:S(2)}) %all-to-all-start.2) | async-done | bytes 1572896 | tf_op jit(solution)/shard_map/all_to_all | solution.py:83
  238.0 4.3 %fusion.27 = bf16[1024,256]{0,1:T(8,128)(2,1)S(1)} fusion(bf16[3072,256]{1,0:T(8,128)(2,1)} %bitcast.12, s32[1024]{0:T(1024)S(1)} %get-tuple-element.52, f32[1024,256]{0,1:T(8,128)} %get-tuple-element.55, f32[1024]{0:T(1024)S(1)} %add_rsqrt_fusion.2), kind=kOutput, calls=%fused_computation.33 | convolution fusion | flops 1615069184 | bytes 3153920 | tf_op jit(solution)/shard_map/dot_general | solution.py:84
  242.2 1.0 copy.14
  (29 shorter events, 1.4 us)
Async XLA Ops:
  0.6 15.7 %copy-start = (bf16[1024,1024]{1,0:T(8,128)(2,1)S(1)}, bf16[1024,1024]{1,0:T(8,128)(2,1)}, u32[]{:S(2)}) copy-start(bf16[1024,1024]{1,0:T(8,128)(2,1)} %param.7) | copy-start | bytes 6291460
  4.8 22.3 %all-to-all-start = ((s32[128,96,1]{1,2,0:T(1,128)}), s32[128,96,1]{1,2,0:T(1,128)S(1)}, u32[]{:S(2)}, u32[]{:S(2)}) async-start(s32[128,96,1]{1,2,0:T(1,128)} %bitcast.2), calls=%async_computation | async-start | bytes 131072 | tf_op jit(solution)/shard_map/all_to_all | solution.py:36
  31.9 86.6 %all-to-all-start.1 = ((bf16[128,96,256]{2,1,0:T(8,128)(2,1)}), bf16[128,96,256]{2,1,0:T(8,128)(2,1)}, u32[]{:S(2)}, u32[]{:S(2)}) async-start(bf16[128,96,256]{2,1,0:T(8,128)(2,1)} %bitcast.36), calls=%async_computation.1 | async-start | bytes 12582912 | tf_op jit(solution)/shard_map/all_to_all | solution.py:57
  192.2 4.8 %copy-start.2 = (f32[3072,256]{1,0:T(8,128)S(1)}, f32[3072,256]{1,0:T(8,128)}, u32[]{:S(2)}) copy-start(f32[3072,256]{1,0:T(8,128)} %convert_element_type.58) | copy-start | bytes 9437188
  205.7 32.2 %all-to-all-start.2 = ((bf16[32,96,256]{2,1,0:T(8,128)(2,1)}), bf16[32,96,256]{2,1,0:T(8,128)(2,1)}, u32[]{:S(2)}, u32[]{:S(2)}) async-start(bf16[32,96,256]{2,1,0:T(8,128)(2,1)} %multiply_convert_fusion.1), calls=%async_computation.2 | async-start | bytes 3145728 | tf_op jit(solution)/shard_map/all_to_all | solution.py:83
  215.2 4.1 %copy-start.1 = (f32[4,1024,256]{2,1,0:T(8,128)S(1)}, f32[4,1024,256]{2,1,0:T(8,128)}, u32[]{:S(2)}) copy-start(f32[4,1024,256]{2,1,0:T(8,128)} %slice.12) | copy-start | bytes 12582916
